TPU v7x, 128 devices: a whole 4x4x4 slice. The times are simulated.
128 devices in a mesh: feat: 8 (over y, core), dom: 16 (over z, x).
Axes of the slice: x: 4, y: 4, z: 4, core: 2. Of those that a mesh axis runs over, the one named last changes fastest.
Arguments:
- features: bfloat16 [768, 262144], P('feat', 'dom'), may hold values from -6 to 6
- neighbours: int32 [65536, 15], P('dom'), may hold values from 0 to 16383
- self_first: bfloat16 [768, 1024], replicated, may hold values from -0.21875 to 0.21875
- neighbour_first: bfloat16 [768, 1024], replicated, may hold values from -0.21875 to 0.21875
- owners: int32 [655360, 1], P(('feat', 'dom')), may hold values from 0 to 15; in each aligned block of 5120 rows (0 to 5119, 5120 to 10239, ...) at most 400 rows name the same one
- offsets: int32 [65536, 10], P(('feat', 'dom')), may hold values from 0 to 511
- self_second: bfloat16 [1024, 1024], replicated, may hold values from -0.1875 to 0.1875
- neighbour_second: bfloat16 [1024, 1024], replicated, may hold values from -0.1875 to 0.1875
- cotangent: bfloat16 [65536, 1024], P(('feat', 'dom')), may hold values from -0.0234375 to 0.0234375
Outputs:
- second_out: bfloat16 [65536, 1024], P(('feat', 'dom'))
- grad_self_second: float32 [1024, 1024], replicated
- grad_neighbour_second: float32 [1024, 1024], replicated
Inputs may be any that keep to these rules, and one draw needn't show every extreme that they name: `owners`: among the 5120 slots of one device (rows of one device), no partition is named more than 400 times, a bound that some block reaches.
All inputs are finite; a program needn't handle non-finite values.
Results may differ from a plain program's by a relative error of at most 0.007.
Values may be sent and summed in bfloat16 or wider, within the bound.
No kernel may reach another device: no remote copies, remote signals or barrier semaphores. Data moves between devices by JAX's collectives and lax.ppermute only.
A program may use at most 192 MiB of HBM per device.

v0:
```python
import jax
import jax.numpy as jnp
from jax import lax
from jax.sharding import PartitionSpec as P


def contract(left, right):
    return lax.dot_general(
        left, right, (((0,), (0,)), ((), ())), preferred_element_type=jnp.float32
    )


def shards(
    features,
    neighbours,
    self_first,
    neighbour_first,
    owners,
    offsets,
    self_second,
    neighbour_second,
    cotangent,
):
    columns_here = features.shape[0]
    targets_part = neighbours.shape[0]
    fanout_first = neighbours.shape[1]
    hidden_width = self_first.shape[1]
    feat_size = lax.axis_size("feat")
    share_rows = targets_part // feat_size
    node_rows = features.T
    gathered = jnp.take(node_rows, neighbours.reshape(-1), axis=0, mode="clip")
    mixed_rows = (
        jnp.sum(
            gathered.reshape(targets_part, fanout_first, columns_here), axis=1, dtype=jnp.float32
        )
        / fanout_first
    ).astype(jnp.bfloat16)
    own_rows = node_rows[:targets_part]
    both = jnp.stack([own_rows, mixed_rows], axis=1).reshape(feat_size, share_rows, 2, columns_here)
    arrived = lax.all_to_all(both, "feat", 0, 0, tiled=True)
    lhs = jnp.transpose(arrived, (1, 0, 2, 3)).reshape(share_rows, -1)
    weights = jnp.stack(
        [
            self_first.reshape(feat_size, columns_here, hidden_width),
            neighbour_first.reshape(feat_size, columns_here, hidden_width),
        ],
        axis=1,
    ).reshape(-1, hidden_width)
    pre_first = jnp.dot(lhs, weights, preferred_element_type=jnp.float32)
    layer_out = jnp.maximum(pre_first, 0.0).astype(jnp.bfloat16)
    seed_rows = cotangent.shape[0]
    fanout_second = offsets.shape[1]
    segment = lax.all_gather(layer_out, "dom", axis=0, tiled=True)
    flat_rows = owners.reshape(seed_rows, fanout_second) * share_rows + offsets
    fetched = jnp.take(segment, flat_rows.reshape(-1), axis=0, mode="clip")
    summed = jnp.sum(
        fetched.reshape(seed_rows, fanout_second, hidden_width), axis=1, dtype=jnp.float32
    )
    mean_second = (summed / fanout_second).astype(jnp.bfloat16)
    second_out = (
        jnp.dot(layer_out, self_second, preferred_element_type=jnp.float32)
        + jnp.dot(mean_second, neighbour_second, preferred_element_type=jnp.float32)
    ).astype(jnp.bfloat16)
    grad_self = contract(layer_out, cotangent)
    grad_neighbour = contract(mean_second, cotangent)
    grad_self, grad_neighbour = lax.psum((grad_self, grad_neighbour), ("feat", "dom"))
    return (second_out, grad_self, grad_neighbour)


def solution(mesh):
    placed = (
        P("feat", "dom"),
        P("dom", None),
        P(),
        P(),
        P(("feat", "dom"), None),
        P(("feat", "dom"), None),
        P(),
        P(),
        P(("feat", "dom"), None),
    )
    return jax.shard_map(
        shards,
        mesh=mesh,
        in_specs=placed,
        out_specs=(P(("feat", "dom"), None), P(), P()),
        check_vma=False,
    )
```

profile of v0, /device:TPU:1, one launch (start us, length us, event | category | flops | bytes accessed | tf_op | source)
XLA Modules:
  0.0 679.6 jit_solution(10008456262759413801)
XLA Ops:
  7.2 0.0 copy-start
  7.2 0.0 all-gather.2.cloned.1.call-start
  7.2 3.0 copy.28
  10.3 3.2 reshape.46
  13.5 5.9 copy.26
  19.4 1.3 slice.8
  20.7 1.2 copy.30
  21.9 208.3 %gather_fusion = bf16[61440,96]{1,0:T(8,128)(2,1)} fusion(bf16[16384,96]{1,0:T(8,128)(2,1)} %bitcast.25, s32[61440]{0:T(1024)S(1)} %broadcast_clamp_fusion), kind=kCustom, calls=%fused_computation | custom fusion | bytes 23838720 | tf_op jit(solution)/shard_map/jit(_take)/gather | solution.py:31
  230.3 26.1 %reshape.42 = f32[4096,15,96]{2,1,0:T(8,128)} reshape(bf16[61440,96]{1,0:T(8,128)(2,1)} %gather_fusion) | data formatting | bytes 35389440 | tf_op jit(solution)/shard_map/convert_element_type | solution.py:33
  256.3 25.2 %reduce_sum.18 = f32[4096,96]{1,0:T(8,128)} reduce(f32[4096,15,96]{2,1,0:T(8,128)} %reshape.42, f32[]{:T(128)} %constant.4.clone.1), dimensions={1}, to_apply=%region_0.1 | reduce | flops 5505024 | bytes 25165828 | tf_op jit(solution)/shard_map/reduce_sum | solution.py:33
  281.5 2.8 copy.29
  284.3 1.5 multiply_convert_fusion.1
  285.8 0.0 copy-start.4
  285.8 0.3 copy.36
  286.1 0.2 copy.31
  286.4 0.6 copy-done.4
  287.0 0.1 pad_maximum_fusion
  287.1 0.0 copy-start.8
  287.1 0.0 copy-start.9
  287.1 26.6 %all_to_all.5 = bf16[8,512,2,96]{1,3,2,0:T(8,128)(2,1)S(1)} all-to-all(bf16[8,512,2,96]{1,3,2,0:T(8,128)(2,1)S(1)} %pad_maximum_fusion), channel_id=1, replica_groups=mesh['feat'=8,'dom'=16] {'feat'}, dimensions={0} | all-to-all | bytes 3145728 | tf_op jit(solution)/shard_map/all_to_all | solution.py:40
  313.7 0.0 copy-done.8
  313.7 0.0 copy-done.9
  313.7 2.8 fusion.4
  316.5 0.0 all-gather.2.cloned.1.call-update
  316.5 0.2 all-reduce.3.cloned.1.call-start
  316.8 0.0 copy-done.6
  316.8 0.1 multiply_reduce_fusion
  316.8 0.2 mul.11
  317.1 0.0 copy-done.5
  317.1 0.9 copy.32
  317.9 1.7 add.10
  319.6 1.1 reshape.54
  320.7 0.0 copy-done.2
  320.8 4.5 fusion.13
  325.3 103.3 %all-gather.2.cloned.1.call-done = bf16[8192,1024]{1,0:T(8,128)(2,1)} async-done(((bf16[512,1024]{1,0:T(8,128)(2,1)}), bf16[8192,1024]{1,0:T(8,128)(2,1)}) %all-gather.2.cloned.1.call-update) | async-done | bytes 16777232 | tf_op jit(solution)/shard_map/all_gather | solution.py:53
  428.6 33.7 %gather_fusion.1 = bf16[5120,1024]{1,0:T(8,128)(2,1)} fusion(bf16[8192,1024]{1,0:T(8,128)(2,1)} %all-gather.2.cloned.1.call-done, s32[5120]{0:T(1024)S(1)} %broadcast_clamp_fusion.1), kind=kCustom, calls=%fused_computation.1 | custom fusion | bytes 20992000 | tf_op jit(solution)/shard_map/jit(_take)/gather | solution.py:55
  462.3 21.4 %reshape.43 = f32[512,10,1024]{2,1,0:T(8,128)} reshape(bf16[5120,1024]{1,0:T(8,128)(2,1)} %gather_fusion.1) | data formatting | bytes 31457280 | tf_op jit(solution)/shard_map/convert_element_type | solution.py:56
  483.7 15.6 %reduce_sum.19 = f32[512,1024]{1,0:T(8,128)} reduce(f32[512,10,1024]{2,1,0:T(8,128)} %reshape.43, f32[]{:T(128)} %constant.4.clone.1), dimensions={1}, to_apply=%region_1.2 | reduce | flops 4718592 | bytes 23068676 | tf_op jit(solution)/shard_map/reduce_sum | solution.py:56
  499.3 5.2 fusion.8
  504.4 0.0 all-reduce.3.cloned.1.call-update
  504.5 0.0 copy-start.7
  504.5 1.3 fusion.12
  505.7 0.3 copy-done.1
  506.1 0.6 copy-done.7
  506.7 2.2 add_convert_fusion
  508.9 156.8 %all-reduce.3.cloned.1.call-done = (f32[1024,1024]{1,0:T(8,128)}, f32[1024,1024]{1,0:T(8,128)}) async-done(((f32[1024,1024]{1,0:T(8,128)}, f32[1024,1024]{1,0:T(8,128)}), (f32[1024,1024]{1,0:T(8,128)}, f32[1024,1024]{1,0:T(8,128)})) %all-reduce.3.cloned.1.call-update) | async-done | bytes 8388624 | tf_op jit(solution)/shard_map/psum | solution.py:66
  665.8 4.9 copy.39
  670.7 2.0 copy.40
  (9 shorter events, 0.1 us)
Async XLA Ops:
  7.2 497.3 %copy-start = (bf16[1024,1024]{1,0:T(8,128)(2,1)S(1)}, bf16[1024,1024]{1,0:T(8,128)(2,1)}, u32[]{:S(2)}) copy-start(bf16[1024,1024]{1,0:T(8,128)(2,1)} %param.15) | copy-start | bytes 6291460
  7.2 421.4 %all-gather.2.cloned.1.call-start = ((), (), s32[]{:S(2)}) async-start(), calls=%async_computation.1 | async-start | bytes 17825792 | tf_op jit(solution)/shard_map/all_gather | solution.py:53
  285.8 1.1 copy-start.4
  287.1 26.6 %copy-start.8 = (bf16[768,1024]{1,0:T(8,128)(2,1)S(1)}, bf16[768,1024]{1,0:T(8,128)(2,1)}, u32[]{:S(2)}) copy-start(bf16[768,1024]{1,0:T(8,128)(2,1)} %param.12) | copy-start | bytes 4718596
  287.1 26.6 %copy-start.9 = (bf16[768,1024]{1,0:T(8,128)(2,1)S(1)}, bf16[768,1024]{1,0:T(8,128)(2,1)}, u32[]{:S(2)}) copy-start(bf16[768,1024]{1,0:T(8,128)(2,1)} %param.11) | copy-start | bytes 4718596
  313.7 3.1 copy-start.6
  313.7 3.4 copy-start.5
  316.5 4.2 copy-start.2
  316.5 349.2 %all-reduce.3.cloned.1.call-start = ((), (), s32[]{:S(2)}) async-start(), calls=%async_computation.2 | async-start | bytes 16777216 | tf_op jit(solution)/shard_map/psum | solution.py:66
  504.5 1.6 copy-start.1
  504.5 2.2 copy-start.7
  665.8 4.9 copy-start.3
Sparse Core Ops, SparseCore 0:
  316.7 111.8 all-gather.1
  504.6 161.1 all-reduce.2
where the time goes:
time: 681 us; the launch traced here: 680 us
  local copies, waits for them, and re-layouts  318 us (47%)
  waiting for transfers between devices  260 us (38%)
  other arithmetic  44.2 us (6%)
  blocking collectives  26.6 us (4%)
  matrix products  16 us (2%)
  between operations  14.2 us (2%)
    gather x1, local copies, waits for them, and re-layouts, shards(): gathered = jnp.take(node_rows, neighbours.reshape(-1), axis=0, mode='clip')  208 us
    psum x1, waiting for transfers between devices, shards(): lax.psum((grad_self, grad_neighbour), ('feat', 'dom'))  157 us
    all_gather x1, waiting for transfers between devices, shards(): segment = lax.all_gather(layer_out, 'dom', axis=0, tiled=True)  103 us
    gather x1, local copies, waits for them, and re-layouts, shards(): fetched = jnp.take(segment, flat_rows.reshape(-1), axis=0, mode='clip')  33.7 us
    all_to_all x1, blocking collectives, shards(): arrived = lax.all_to_all(both, 'feat', 0, 0, tiled=True)  26.6 us
    convert_element_type x1, local copies, waits for them, and re-layouts, shards(): jnp.sum(gathered.reshape(targets_part, fanout_first, columns_here), axis=...  26.1 us
    reduce_sum x1, other arithmetic, shards(): jnp.sum(gathered.reshape(targets_part, fanout_first, columns_here), axis=...  25.2 us
    convert_element_type x1, local copies, waits for them, and re-layouts, shards(): jnp.sum(fetched.reshape(seed_rows, fanout_second, hidden_width), axis=1,...  21.4 us
  transfers between devices with their start and end apart: 2, of which 2 were waited for; matrix products, arithmetic and copies ran while one was open for 2% of the time, Pallas kernels for 0%

commit v1 on v0

--- a/solution.py
+++ b/solution.py
@@ -2,6 +2,12 @@
 import jax.numpy as jnp
 from jax import lax
 from jax.sharding import PartitionSpec as P
+
+
+def keep_up_zone(z_in, where_dim):
+    val2 = list(z_in.shape[1:])
+    val2[where_dim] *= z_in.shape[0]
+    return jnp.moveaxis(z_in, 0, where_dim).reshape(val2)
 
 
 def contract(left, right):
@@ -50,7 +56,23 @@
     layer_out = jnp.maximum(pre_first, 0.0).astype(jnp.bfloat16)
     seed_rows = cotangent.shape[0]
     fanout_second = offsets.shape[1]
-    segment = lax.all_gather(layer_out, "dom", axis=0, tiled=True)
+    parts_n = lax.axis_size("dom")
+    trail = [(it, (it + 1) % parts_n) for it in range(parts_n)]
+    frames = [(t, q) for q, t in trail]
+    kept_arr, block_out = ([], [])
+    for at in range(parts_n - 1):
+        if at % 2 == 0:
+            part_next = lax.ppermute(kept_arr[-1] if kept_arr else layer_out, "dom", trail)
+            kept_arr.append(part_next)
+        else:
+            wide_out = lax.ppermute(block_out[-1] if block_out else layer_out, "dom", frames)
+            block_out.append(wide_out)
+    inter = jnp.stack([*kept_arr[::-1], layer_out, *block_out], axis=0)
+    y_new = len(kept_arr)
+    clean = lax.axis_index("dom")
+    f_now = clean - y_new
+    inter = inter[(jnp.arange(parts_n) - f_now) % parts_n]
+    segment = keep_up_zone(inter, 0)
     flat_rows = owners.reshape(seed_rows, fanout_second) * share_rows + offsets
     fetched = jnp.take(segment, flat_rows.reshape(-1), axis=0, mode="clip")
     summed = jnp.sum(

time: 681 us -> 808 us (1.19)
  waiting for transfers between devices: 260 us -> 310 us
  local copies, waits for them, and re-layouts: 318 us -> 354 us
  starting transfers between devices: 0.26 us -> 36.2 us
    ppermute x0 -> x15, waiting for transfers between devices: none -> 150 us  [the longest x8 150 us: shards(): lax.ppermute(kept_arr[-1] if kept_arr else layer_out, 'dom', trail)]
    all_gather x1 -> x0, waiting for transfers between devices: 103 us -> none  [shards(): segment = lax.all_gather(layer_out, 'dom', axis=0, tiled=True)]
    ppermute x0 -> x15, starting transfers between devices: none -> 36.1 us  [the longest x7 34.9 us: shards(): lax.ppermute(block_out[-1] if block_out else layer_out, 'dom', frames)]
    unnamed x26 -> x69, local copies, waits for them, and re-layouts: 18.6 us -> 39.1 us
    gather x0 -> x1, local copies, waits for them, and re-layouts: none -> 13 us  [shards(): inter = inter[(jnp.arange(parts_n) - f_now) % parts_n]]
  transfers between devices with their start and end apart: 2 -> 16, of which waited for: 2 -> 9; matrix products, arithmetic and copies ran while one was open for 2% -> 4% of each run, Pallas kernels for 0% -> 0%
where the time goes in v1:
time: 808 us; the launch traced here: 806 us
  local copies, waits for them, and re-layouts  354 us (44%)
  waiting for transfers between devices  310 us (38%)
  other arithmetic  45.6 us (6%)
  starting transfers between devices  36.2 us (4%)
  blocking collectives  26.3 us (3%)
  matrix products  19.2 us (2%)
  between operations  14.3 us (2%)
    gather x1, local copies, waits for them, and re-layouts, shards(): gathered = jnp.take(node_rows, neighbours.reshape(-1), axis=0, mode='clip')  209 us
    psum x1, waiting for transfers between devices, shards(): lax.psum((grad_self, grad_neighbour), ('feat', 'dom'))  160 us
    ppermute x8, waiting for transfers between devices, shards(): lax.ppermute(kept_arr[-1] if kept_arr else layer_out, 'dom', trail)  150 us
    unnamed x69, local copies, waits for them, and re-layouts  39.1 us
    ppermute x7, starting transfers between devices, shards(): lax.ppermute(block_out[-1] if block_out else layer_out, 'dom', frames)  34.9 us
    gather x1, local copies, waits for them, and re-layouts, shards(): fetched = jnp.take(segment, flat_rows.reshape(-1), axis=0, mode='clip')  33.8 us
    all_to_all x1, blocking collectives, shards(): arrived = lax.all_to_all(both, 'feat', 0, 0, tiled=True)  26.3 us
    convert_element_type x1, local copies, waits for them, and re-layouts, shards(): jnp.sum(gathered.reshape(targets_part, fanout_first, columns_here), axis=...  26.1 us
  transfers between devices with their start and end apart: 16, of which 9 were waited for; matrix products, arithmetic and copies ran while one was open for 4% of the time, Pallas kernels for 0%

profile of v1, /device:TPU:1, one launch (start us, length us, event | category | flops | bytes accessed | tf_op | source)
XLA Modules:
  0.0 805.8 jit_solution(9287065512135525611)
XLA Ops:
  7.2 6.0 copy.26
  13.2 2.9 copy.28
  16.1 3.2 reshape.99
  19.4 1.3 slice.10
  20.7 208.5 %gather_fusion = bf16[61440,96]{1,0:T(8,128)(2,1)} fusion(bf16[16384,96]{1,0:T(8,128)(2,1)} %bitcast.60, s32[61440]{0:T(1024)S(1)} %broadcast_clamp_fusion), kind=kCustom, calls=%fused_computation | custom fusion | bytes 23838720 | tf_op jit(solution)/shard_map/jit(_take)/gather | solution.py:37
  229.2 26.1 %reshape.95 = f32[4096,15,96]{2,1,0:T(8,128)} reshape(bf16[61440,96]{1,0:T(8,128)(2,1)} %gather_fusion) | data formatting | bytes 35389440 | tf_op jit(solution)/shard_map/convert_element_type | solution.py:39
  255.3 25.2 %reduce_sum.18 = f32[4096,96]{1,0:T(8,128)} reduce(f32[4096,15,96]{2,1,0:T(8,128)} %reshape.95, f32[]{:T(128)} %constant.12.clone.1), dimensions={1}, to_apply=%region_0.1 | reduce | flops 5505024 | bytes 25165828 | tf_op jit(solution)/shard_map/reduce_sum | solution.py:39
  280.4 2.8 copy.29
  283.2 1.5 multiply_convert_fusion.1
  285.1 1.1 copy.31
  286.2 1.2 copy.30
  287.4 1.5 pad_maximum_fusion
  288.9 26.3 %all_to_all.5 = bf16[8,512,2,96]{1,3,2,0:T(8,128)(2,1)S(1)} all-to-all(bf16[8,512,2,96]{1,3,2,0:T(8,128)(2,1)S(1)} %pad_maximum_fusion), channel_id=1, replica_groups=mesh['feat'=8,'dom'=16] {'feat'}, dimensions={0} | all-to-all | bytes 3145728 | tf_op jit(solution)/shard_map/all_to_all | solution.py:46
  315.3 3.7 fusion.4
  318.9 1.3 collective-permute-start
  320.2 27.2 %collective-permute-done = bf16[512,1024]{1,0:T(8,128)(2,1)S(1)} collective-permute-done((bf16[512,1024]{1,0:T(8,128)(2,1)S(1)}, bf16[512,1024]{1,0:T(8,128)(2,1)S(1)}, u32[]{:S(2)}, u32[]{:S(2)}) %collective-permute-start) | collective-permute-done | bytes 1048608 | tf_op jit(solution)/shard_map/ppermute | solution.py:65
  347.5 4.8 collective-permute-start.8
  352.2 21.6 %collective-permute-done.1 = bf16[512,1024]{1,0:T(8,128)(2,1)S(1)} collective-permute-done((bf16[512,1024]{1,0:T(8,128)(2,1)S(1)}, bf16[512,1024]{1,0:T(8,128)(2,1)S(1)}, u32[]{:S(2)}, u32[]{:S(2)}) %collective-permute-start.1) | collective-permute-done | bytes 1048608 | tf_op jit(solution)/shard_map/ppermute | solution.py:65
  373.9 4.8 collective-permute-start.9
  378.7 20.7 %collective-permute-done.2 = bf16[512,1024]{1,0:T(8,128)(2,1)S(1)} collective-permute-done((bf16[512,1024]{1,0:T(8,128)(2,1)S(1)}, bf16[512,1024]{1,0:T(8,128)(2,1)S(1)}, u32[]{:S(2)}, u32[]{:S(2)}) %collective-permute-start.2) | collective-permute-done | bytes 1048608 | tf_op jit(solution)/shard_map/ppermute | solution.py:65
  399.5 5.0 collective-permute-start.10
  404.5 19.7 %collective-permute-done.3 = bf16[512,1024]{1,0:T(8,128)(2,1)S(1)} collective-permute-done((bf16[512,1024]{1,0:T(8,128)(2,1)S(1)}, bf16[512,1024]{1,0:T(8,128)(2,1)S(1)}, u32[]{:S(2)}, u32[]{:S(2)}) %collective-permute-start.3) | collective-permute-done | bytes 1048608 | tf_op jit(solution)/shard_map/ppermute | solution.py:65
  424.2 4.8 collective-permute-start.11
  429.0 19.0 %collective-permute-done.4 = bf16[512,1024]{1,0:T(8,128)(2,1)S(1)} collective-permute-done((bf16[512,1024]{1,0:T(8,128)(2,1)S(1)}, bf16[512,1024]{1,0:T(8,128)(2,1)S(1)}, u32[]{:S(2)}, u32[]{:S(2)}) %collective-permute-start.4) | collective-permute-done | bytes 1048608 | tf_op jit(solution)/shard_map/ppermute | solution.py:65
  449.1 4.8 collective-permute-start.12
  453.8 17.2 %collective-permute-done.5 = bf16[512,1024]{1,0:T(8,128)(2,1)S(1)} collective-permute-done((bf16[512,1024]{1,0:T(8,128)(2,1)S(1)}, bf16[512,1024]{1,0:T(8,128)(2,1)S(1)}, u32[]{:S(2)}, u32[]{:S(2)}) %collective-permute-start.5) | collective-permute-done | bytes 1048608 | tf_op jit(solution)/shard_map/ppermute | solution.py:65
  471.0 5.6 collective-permute-start.13
  476.6 16.6 %collective-permute-done.6 = bf16[512,1024]{1,0:T(8,128)(2,1)} collective-permute-done((bf16[512,1024]{1,0:T(8,128)(2,1)S(1)}, bf16[512,1024]{1,0:T(8,128)(2,1)}, u32[]{:S(2)}, u32[]{:S(2)}) %collective-permute-start.6) | collective-permute-done | bytes 1048608 | tf_op jit(solution)/shard_map/ppermute | solution.py:65
  494.4 1.7 add.36
  496.1 1.1 reshape.115
  497.3 4.7 fusion.15
  502.0 5.1 collective-permute-start.14
  507.1 7.8 collective-permute-done.7
  514.9 2.3 bitcast_dynamic-update-slice_fusion.15
  517.2 2.4 bitcast_dynamic-update-slice_fusion.14
  524.8 1.1 bitcast_dynamic-update-slice_fusion.8
  531.3 2.3 bitcast_dynamic-update-slice_fusion.2
  533.6 2.3 bitcast_dynamic-update-slice_fusion.1
  537.0 13.0 %gather_fusion.1 = bf16[16,512,1024]{2,1,0:T(8,128)(2,1)} fusion(bf16[16,512,1024]{2,1,0:T(8,128)(2,1)} %bitcast_dynamic-update-slice_fusion, s32[1024]{0:T(1024)S(1)} %pad_clamp_fusion), kind=kCustom, calls=%fused_computation.1 | custom fusion | bytes 33554496 | tf_op jit(solution)/shard_map/gather | solution.py:74
  550.0 33.8 %gather_fusion.2 = bf16[5120,1024]{1,0:T(8,128)(2,1)} fusion(bf16[8192,1024]{1,0:T(8,128)(2,1)} %bitcast.61, s32[5120]{0:T(1024)S(1)} %broadcast_clamp_fusion.1), kind=kCustom, calls=%fused_computation.2 | custom fusion | bytes 20992000 | tf_op jit(solution)/shard_map/jit(_take)/gather | solution.py:77
  583.8 21.5 %reshape.96 = f32[512,10,1024]{2,1,0:T(8,128)} reshape(bf16[5120,1024]{1,0:T(8,128)(2,1)} %gather_fusion.2) | data formatting | bytes 31457280 | tf_op jit(solution)/shard_map/convert_element_type | solution.py:78
  605.3 15.6 %reduce_sum.19 = f32[512,1024]{1,0:T(8,128)} reduce(f32[512,10,1024]{2,1,0:T(8,128)} %reshape.96, f32[]{:T(128)} %constant.12.clone.1), dimensions={1}, to_apply=%region_1.2 | reduce | flops 4718592 | bytes 23068676 | tf_op jit(solution)/shard_map/reduce_sum | solution.py:78
  620.8 5.2 fusion.8
  626.0 1.3 fusion.14
  627.3 4.5 add_convert_fusion
  631.7 160.2 %all-reduce.3.cloned.1.call-done = (f32[1024,1024]{1,0:T(8,128)}, f32[1024,1024]{1,0:T(8,128)}) async-done(((f32[1024,1024]{1,0:T(8,128)}, f32[1024,1024]{1,0:T(8,128)}), (f32[1024,1024]{1,0:T(8,128)}, f32[1024,1024]{1,0:T(8,128)})) %all-reduce.3.cloned.1.call-update) | async-done | bytes 8388624 | tf_op jit(solution)/shard_map/psum | solution.py:88
  792.0 4.9 copy.54
  796.9 2.0 copy.55
  (83 shorter events, 14.4 us)
Async XLA Ops:
  7.2 618.9 %copy-start = (bf16[1024,1024]{1,0:T(8,128)(2,1)S(1)}, bf16[1024,1024]{1,0:T(8,128)(2,1)}, u32[]{:S(2)}) copy-start(bf16[1024,1024]{1,0:T(8,128)(2,1)} %param.15) | copy-start | bytes 6291460
  7.2 784.8 %all-reduce.3.cloned.1.call-start = ((), (), s32[]{:S(2)}) async-start(), calls=%async_computation.1 | async-start | bytes 16777216 | tf_op jit(solution)/shard_map/psum | solution.py:88
  283.2 210.1 %copy-start.23 = (s32[5120,1]{0,1:T(1,128)S(1)}, s32[5120,1]{0,1:T(1,128)}, u32[]{:S(2)}) copy-start(s32[5120,1]{0,1:T(1,128)} %param.13) | copy-start | bytes 61444
  284.8 208.8 %copy-start.22 = (s32[512,10]{0,1:T(8,128)S(1)}, s32[512,10]{0,1:T(8,128)}, u32[]{:S(2)}) copy-start(s32[512,10]{0,1:T(8,128)} %param.14) | copy-start | bytes 61444
  318.9 28.5 %collective-permute-start = (bf16[512,1024]{1,0:T(8,128)(2,1)S(1)}, bf16[512,1024]{1,0:T(8,128)(2,1)S(1)}, u32[]{:S(2)}, u32[]{:S(2)}) collective-permute-start(bf16[512,1024]{1,0:T(8,128)(2,1)S(1)} %fusion.4), channel_id=1, source_target_pairs={{0,1},{1,2},{2,3},{3,4},{4,5},{5,6},{6,7},{7,8},{8,9},{9,10},{10,1... | collective-permute-start | bytes 3145736 | tf_op jit(solution)/shard_map/ppermute | solution.py:65
  347.5 26.4 %copy-start.2 = (bf16[512,1024]{1,0:T(8,128)(2,1)}, bf16[512,1024]{1,0:T(8,128)(2,1)S(1)}, u32[]{:S(2)}) copy-start(bf16[512,1024]{1,0:T(8,128)(2,1)S(1)} %collective-permute-done) | copy-start | bytes 3145732
  347.5 26.4 %collective-permute-start.1 = (bf16[512,1024]{1,0:T(8,128)(2,1)S(1)}, bf16[512,1024]{1,0:T(8,128)(2,1)S(1)}, u32[]{:S(2)}, u32[]{:S(2)}) collective-permute-start(bf16[512,1024]{1,0:T(8,128)(2,1)S(1)} %collective-permute-done), channel_id=1, source_target_pairs={{0,1},{1,2},{2,3},{3,4},{4,5},{5,6},{6,7},{7,8},{8,9},{9,10},{10,1... | collective-permute-start | bytes 3145736 | tf_op jit(solution)/shard_map/ppermute | solution.py:65
  347.5 26.4 %collective-permute-start.8 = (bf16[512,1024]{1,0:T(8,128)(2,1)S(1)}, bf16[512,1024]{1,0:T(8,128)(2,1)S(1)}, u32[]{:S(2)}, u32[]{:S(2)}) collective-permute-start(bf16[512,1024]{1,0:T(8,128)(2,1)S(1)} %fusion.4), channel_id=1, source_target_pairs={{1,0},{2,1},{3,2},{4,3},{5,4},{6,5},{7,6},{8,7},{9,8},{10,9},{11,1... | collective-permute-start | bytes 3145736 | tf_op jit(solution)/shard_map/ppermute | solution.py:68
  373.9 25.6 %copy-start.6 = (bf16[512,1024]{1,0:T(8,128)(2,1)}, bf16[512,1024]{1,0:T(8,128)(2,1)S(1)}, u32[]{:S(2)}) copy-start(bf16[512,1024]{1,0:T(8,128)(2,1)S(1)} %collective-permute-done.1) | copy-start | bytes 3145732
  373.9 25.6 %collective-permute-start.2 = (bf16[512,1024]{1,0:T(8,128)(2,1)S(1)}, bf16[512,1024]{1,0:T(8,128)(2,1)S(1)}, u32[]{:S(2)}, u32[]{:S(2)}) collective-permute-start(bf16[512,1024]{1,0:T(8,128)(2,1)S(1)} %collective-permute-done.1), channel_id=1, source_target_pairs={{0,1},{1,2},{2,3},{3,4},{4,5},{5,6},{6,7},{7,8},{8,9},{9,10},{10,1... | collective-permute-start | bytes 3145736 | tf_op jit(solution)/shard_map/ppermute | solution.py:65
  373.9 4.8 copy-start.4
  373.9 25.5 %collective-permute-start.9 = (bf16[512,1024]{1,0:T(8,128)(2,1)S(1)}, bf16[512,1024]{1,0:T(8,128)(2,1)S(1)}, u32[]{:S(2)}, u32[]{:S(2)}) collective-permute-start(bf16[512,1024]{1,0:T(8,128)(2,1)S(1)} %collective-permute-done.8), channel_id=1, source_target_pairs={{1,0},{2,1},{3,2},{4,3},{5,4},{6,5},{7,6},{8,7},{9,8},{10,9},{11,1... | collective-permute-start | bytes 3145736 | tf_op jit(solution)/shard_map/ppermute | solution.py:68
  399.4 24.7 %copy-start.10 = (bf16[512,1024]{1,0:T(8,128)(2,1)}, bf16[512,1024]{1,0:T(8,128)(2,1)S(1)}, u32[]{:S(2)}) copy-start(bf16[512,1024]{1,0:T(8,128)(2,1)S(1)} %collective-permute-done.2) | copy-start | bytes 3145732
  399.4 24.7 %collective-permute-start.3 = (bf16[512,1024]{1,0:T(8,128)(2,1)S(1)}, bf16[512,1024]{1,0:T(8,128)(2,1)S(1)}, u32[]{:S(2)}, u32[]{:S(2)}) collective-permute-start(bf16[512,1024]{1,0:T(8,128)(2,1)S(1)} %collective-permute-done.2), channel_id=1, source_target_pairs={{0,1},{1,2},{2,3},{3,4},{4,5},{5,6},{6,7},{7,8},{8,9},{9,10},{10,1... | collective-permute-start | bytes 3145736 | tf_op jit(solution)/shard_map/ppermute | solution.py:65
  399.5 5.0 copy-start.8
  399.5 24.7 %collective-permute-start.10 = (bf16[512,1024]{1,0:T(8,128)(2,1)S(1)}, bf16[512,1024]{1,0:T(8,128)(2,1)S(1)}, u32[]{:S(2)}, u32[]{:S(2)}) collective-permute-start(bf16[512,1024]{1,0:T(8,128)(2,1)S(1)} %collective-permute-done.9), channel_id=1, source_target_pairs={{1,0},{2,1},{3,2},{4,3},{5,4},{6,5},{7,6},{8,7},{9,8},{10,9},{11,1... | collective-permute-start | bytes 3145736 | tf_op jit(solution)/shard_map/ppermute | solution.py:68
  424.2 46.9 %copy-start.16 = (bf16[512,1024]{1,0:T(8,128)(2,1)}, bf16[512,1024]{1,0:T(8,128)(2,1)S(1)}, u32[]{:S(2)}) copy-start(bf16[512,1024]{1,0:T(8,128)(2,1)S(1)} %collective-permute-done.3) | copy-start | bytes 3145732
  424.2 23.9 %collective-permute-start.4 = (bf16[512,1024]{1,0:T(8,128)(2,1)S(1)}, bf16[512,1024]{1,0:T(8,128)(2,1)S(1)}, u32[]{:S(2)}, u32[]{:S(2)}) collective-permute-start(bf16[512,1024]{1,0:T(8,128)(2,1)S(1)} %collective-permute-done.3), channel_id=1, source_target_pairs={{0,1},{1,2},{2,3},{3,4},{4,5},{5,6},{6,7},{7,8},{8,9},{9,10},{10,1... | collective-permute-start | bytes 3145736 | tf_op jit(solution)/shard_map/ppermute | solution.py:65
  424.2 4.8 copy-start.12
  424.2 23.8 %collective-permute-start.11 = (bf16[512,1024]{1,0:T(8,128)(2,1)S(1)}, bf16[512,1024]{1,0:T(8,128)(2,1)S(1)}, u32[]{:S(2)}, u32[]{:S(2)}) collective-permute-start(bf16[512,1024]{1,0:T(8,128)(2,1)S(1)} %collective-permute-done.10), channel_id=1, source_target_pairs={{1,0},{2,1},{3,2},{4,3},{5,4},{6,5},{7,6},{8,7},{9,8},{10,9},{11,1... | collective-permute-start | bytes 3145736 | tf_op jit(solution)/shard_map/ppermute | solution.py:68
  448.0 28.6 %copy-start.18 = (bf16[512,1024]{1,0:T(8,128)(2,1)}, bf16[512,1024]{1,0:T(8,128)(2,1)S(1)}, u32[]{:S(2)}) copy-start(bf16[512,1024]{1,0:T(8,128)(2,1)S(1)} %collective-permute-done.4) | copy-start | bytes 3145732
  448.0 23.0 %collective-permute-start.5 = (bf16[512,1024]{1,0:T(8,128)(2,1)S(1)}, bf16[512,1024]{1,0:T(8,128)(2,1)S(1)}, u32[]{:S(2)}, u32[]{:S(2)}) collective-permute-start(bf16[512,1024]{1,0:T(8,128)(2,1)S(1)} %collective-permute-done.4), channel_id=1, source_target_pairs={{0,1},{1,2},{2,3},{3,4},{4,5},{5,6},{6,7},{7,8},{8,9},{9,10},{10,1... | collective-permute-start | bytes 3145736 | tf_op jit(solution)/shard_map/ppermute | solution.py:65
  448.0 1.0 copy-start.14
  449.1 22.0 %collective-permute-start.12 = (bf16[512,1024]{1,0:T(8,128)(2,1)S(1)}, bf16[512,1024]{1,0:T(8,128)(2,1)}, u32[]{:S(2)}, u32[]{:S(2)}) collective-permute-start(bf16[512,1024]{1,0:T(8,128)(2,1)S(1)} %collective-permute-done.11), channel_id=1, source_target_pairs={{1,0},{2,1},{3,2},{4,3},{5,4},{6,5},{7,6},{8,7},{9,8},{10,9},{11,1... | collective-permute-start | bytes 3145736 | tf_op jit(solution)/shard_map/ppermute | solution.py:68
  471.0 22.3 %copy-start.20 = (bf16[512,1024]{1,0:T(8,128)(2,1)}, bf16[512,1024]{1,0:T(8,128)(2,1)S(1)}, u32[]{:S(2)}) copy-start(bf16[512,1024]{1,0:T(8,128)(2,1)S(1)} %collective-permute-done.5) | copy-start | bytes 3145732
  471.0 22.2 %collective-permute-start.6 = (bf16[512,1024]{1,0:T(8,128)(2,1)S(1)}, bf16[512,1024]{1,0:T(8,128)(2,1)}, u32[]{:S(2)}, u32[]{:S(2)}) collective-permute-start(bf16[512,1024]{1,0:T(8,128)(2,1)S(1)} %collective-permute-done.5), channel_id=1, source_target_pairs={{0,1},{1,2},{2,3},{3,4},{4,5},{5,6},{6,7},{7,8},{8,9},{9,10},{10,1... | collective-permute-start | bytes 3145736 | tf_op jit(solution)/shard_map/ppermute | solution.py:65
  471.0 31.0 %collective-permute-start.13 = (bf16[512,1024]{1,0:T(8,128)(2,1)}, bf16[512,1024]{1,0:T(8,128)(2,1)}, u32[]{:S(2)}, u32[]{:S(2)}) collective-permute-start(bf16[512,1024]{1,0:T(8,128)(2,1)} %collective-permute-done.12), channel_id=1, source_target_pairs={{1,0},{2,1},{3,2},{4,3},{5,4},{6,5},{7,6},{8,7},{9,8},{10,9},{11,1... | collective-permute-start | bytes 3145736 | tf_op jit(solution)/shard_map/ppermute | solution.py:68
  493.3 21.6 %collective-permute-start.7 = (bf16[512,1024]{1,0:T(8,128)(2,1)}, bf16[512,1024]{1,0:T(8,128)(2,1)}, u32[]{:S(2)}, u32[]{:S(2)}) collective-permute-start(bf16[512,1024]{1,0:T(8,128)(2,1)} %collective-permute-done.6), channel_id=1, source_target_pairs={{0,1},{1,2},{2,3},{3,4},{4,5},{5,6},{6,7},{7,8},{8,9},{9,10},{10,1... | collective-permute-start | bytes 3145736 | tf_op jit(solution)/shard_map/ppermute | solution.py:65
  497.2 22.3 %copy-start.21 = (bf16[512,1024]{1,0:T(8,128)(2,1)S(1)}, bf16[512,1024]{1,0:T(8,128)(2,1)}, u32[]{:S(2)}) copy-start(bf16[512,1024]{1,0:T(8,128)(2,1)} %copy-done.20) | copy-start | bytes 3145732
  497.2 23.3 %copy-start.19 = (bf16[512,1024]{1,0:T(8,128)(2,1)S(1)}, bf16[512,1024]{1,0:T(8,128)(2,1)}, u32[]{:S(2)}) copy-start(bf16[512,1024]{1,0:T(8,128)(2,1)} %copy-done.18) | copy-start | bytes 3145732
  497.2 24.4 %copy-start.17 = (bf16[512,1024]{1,0:T(8,128)(2,1)S(1)}, bf16[512,1024]{1,0:T(8,128)(2,1)}, u32[]{:S(2)}) copy-start(bf16[512,1024]{1,0:T(8,128)(2,1)} %copy-done.16) | copy-start | bytes 3145732
  497.3 25.5 %copy-start.11 = (bf16[512,1024]{1,0:T(8,128)(2,1)S(1)}, bf16[512,1024]{1,0:T(8,128)(2,1)}, u32[]{:S(2)}) copy-start(bf16[512,1024]{1,0:T(8,128)(2,1)} %copy-done.10) | copy-start | bytes 3145732
  497.3 26.5 %copy-start.7 = (bf16[512,1024]{1,0:T(8,128)(2,1)S(1)}, bf16[512,1024]{1,0:T(8,128)(2,1)}, u32[]{:S(2)}) copy-start(bf16[512,1024]{1,0:T(8,128)(2,1)} %copy-done.6) | copy-start | bytes 3145732
  497.3 27.5 %copy-start.3 = (bf16[512,1024]{1,0:T(8,128)(2,1)S(1)}, bf16[512,1024]{1,0:T(8,128)(2,1)}, u32[]{:S(2)}) copy-start(bf16[512,1024]{1,0:T(8,128)(2,1)} %copy-done.2) | copy-start | bytes 3145732
  502.0 25.0 %copy-start.5 = (bf16[512,1024]{1,0:T(8,128)(2,1)S(1)}, bf16[512,1024]{1,0:T(8,128)(2,1)}, u32[]{:S(2)}) copy-start(bf16[512,1024]{1,0:T(8,128)(2,1)} %copy-done.4) | copy-start | bytes 3145732
  502.0 26.1 %copy-start.9 = (bf16[512,1024]{1,0:T(8,128)(2,1)S(1)}, bf16[512,1024]{1,0:T(8,128)(2,1)}, u32[]{:S(2)}) copy-start(bf16[512,1024]{1,0:T(8,128)(2,1)} %copy-done.8) | copy-start | bytes 3145732
  502.0 33.9 %collective-permute-start.14 = (bf16[512,1024]{1,0:T(8,128)(2,1)}, bf16[512,1024]{1,0:T(8,128)(2,1)S(1)}, u32[]{:S(2)}, u32[]{:S(2)}) collective-permute-start(bf16[512,1024]{1,0:T(8,128)(2,1)} %collective-permute-done.13), channel_id=1, source_target_pairs={{1,0},{2,1},{3,2},{4,3},{5,4},{6,5},{7,6},{8,7},{9,8},{10,9},{11,1... | collective-permute-start | bytes 3145736 | tf_op jit(solution)/shard_map/ppermute | solution.py:68
  517.2 12.0 %copy-start.13 = (bf16[512,1024]{1,0:T(8,128)(2,1)S(1)}, bf16[512,1024]{1,0:T(8,128)(2,1)}, u32[]{:S(2)}) copy-start(bf16[512,1024]{1,0:T(8,128)(2,1)} %copy-done.12) | copy-start | bytes 3145732
  519.5 10.7 %copy-start.15 = (bf16[512,1024]{1,0:T(8,128)(2,1)S(1)}, bf16[512,1024]{1,0:T(8,128)(2,1)}, u32[]{:S(2)}) copy-start(bf16[512,1024]{1,0:T(8,128)(2,1)} %copy-done.14) | copy-start | bytes 3145732
  792.0 4.9 copy-start.1
Sparse Core Ops, SparseCore 0:
  626.1 165.7 all-reduce.2
